TPU v7x, 32 devices: a whole 2x2x4 slice. The times are simulated.
32 devices in a mesh: dp: 4 (over y, x), seq: 8 (over z, core).
Axes of the slice: x: 2, y: 2, z: 4, core: 2. Of those that a mesh axis runs over, the one named last changes fastest.
Arguments:
- asking_vectors_matrix: bfloat16 [4, 1024, 2048], P('dp', 'seq'), may hold values from -6 to 6
- matched_keys_matrix: bfloat16 [4, 1024, 2048], P('dp', 'seq'), may hold values from -6 to 6
- carried_vectors_matrix: bfloat16 [4, 1024, 2048], P('dp', 'seq'), may hold values from -6 to 6
- upstream_cotangent: bfloat16 [4, 1024, 2048], P('dp', 'seq'), may hold values from -6 to 6
- w_out: bfloat16 [2048, 2048], P('seq'), may hold values from -0.125 to 0.125
- panel_entry_offsets: int32 [4, 9], P('dp'), may hold values from 0 to 32, as said below
- rightward_panel_per_entry: int32 [4, 32], P('dp'), may hold values from 0 to 7, as said below
Outputs:
- layer_out: bfloat16 [4, 1024, 2048], P('dp', 'seq')
- q_grad: bfloat16 [4, 1024, 2048], P('dp', 'seq')
- k_grad: bfloat16 [4, 1024, 2048], P('dp', 'seq')
- v_grad: bfloat16 [4, 1024, 2048], P('dp', 'seq')
- w_out_grad: float32 [2048, 2048], P('seq')
Inputs may be any that keep to these rules, and one draw needn't show every extreme that they name: panel_entry_offsets[b, 0] is 0 and panel_entry_offsets never falls along a row; tile row r owns slots panel_entry_offsets[b, r] to panel_entry_offsets[b, r + 1] - 1, 1 to 8 of them, and its own tile r is among its blocks; in every subgraph one tile row holds all 8 tiles; panel_entry_offsets[b, 8], the used slots, lies between 16 and 32 and equals 32 for at least one subgraph. `rightward_panel_per_entry`: the slots of a tile row hold distinct column tiles in rising order; slots from panel_entry_offsets[b, 8] on hold arbitrary tile numbers that take no part.
All inputs are finite; a program needn't handle non-finite values.
Results may differ from a plain program's by a relative error of at most 0.034.
Values may be sent and summed in bfloat16 or wider, within the bound.
No kernel may reach another device: no remote copies, remote signals or barrier semaphores. Data moves between devices by JAX's collectives and lax.ppermute only.
A program may use at most 128 MiB of HBM per device.

v0:
```python
import math
import jax
import jax.numpy as jnp
from jax import lax
from jax.sharding import PartitionSpec as P

H = 16
HD = 128


def tile_mask(starts, columns, nodes):
    tile_count = starts.shape[0] - 1
    slot_count = columns.shape[0]
    tile_size = nodes // tile_count
    slot_index = jnp.arange(slot_count, dtype=jnp.int32)
    entry_row = jnp.sum((starts[1:][None, :] <= slot_index[:, None]).astype(jnp.int32), axis=1)
    tile_ids = jnp.arange(tile_count, dtype=jnp.int32)
    row_hot = (entry_row[:, None] == tile_ids[None, :]).astype(jnp.int32)
    col_hot = (columns[:, None] == tile_ids[None, :]).astype(jnp.int32)
    pairs = jnp.einsum("er,ec->rc", row_hot, col_hot) > 0
    full = jnp.broadcast_to(pairs[:, None, :, None], (tile_count, tile_size, tile_count, tile_size))
    return full.reshape(nodes, nodes)


def attend(q, k, v, g, allowed):
    factor = 1.0 / math.sqrt(q.shape[-1])
    scores = jnp.einsum("ihd,jhd->hij", q, k, preferred_element_type=jnp.float32) * factor
    masked = jnp.where(allowed[None], scores, -jnp.inf)
    row_max = jnp.max(masked, axis=2, keepdims=True)
    expd = jnp.where(allowed[None], jnp.exp(scores - row_max), 0.0)
    row_total = jnp.sum(expd, axis=2, keepdims=True)
    weighted = jnp.einsum(
        "hij,jhd->ihd", expd.astype(jnp.bfloat16), v, preferred_element_type=jnp.float32
    )
    totals = jnp.transpose(row_total[:, :, 0])[:, :, None]
    attended = (weighted / totals).astype(jnp.bfloat16)
    return (attended, expd, row_total)


def attend_back(q, k, v, g, attended, expd, row_total):
    factor = 1.0 / math.sqrt(q.shape[-1])
    prob = expd / row_total
    prob_low = prob.astype(jnp.bfloat16)
    v_grad = jnp.einsum("hij,ihd->jhd", prob_low, g, preferred_element_type=jnp.float32)
    prob_grad = jnp.einsum("ihd,jhd->hij", g, v, preferred_element_type=jnp.float32)
    delta = jnp.sum(attended.astype(jnp.float32) * g.astype(jnp.float32), axis=2)
    delta = jnp.transpose(delta)[:, :, None]
    score_grad = (prob * (prob_grad - delta) * factor).astype(jnp.bfloat16)
    q_grad = jnp.einsum("hij,jhd->ihd", score_grad, k, preferred_element_type=jnp.float32)
    k_grad = jnp.einsum("hij,ihd->jhd", score_grad, q, preferred_element_type=jnp.float32)
    return (q_grad.astype(jnp.bfloat16), k_grad.astype(jnp.bfloat16), v_grad.astype(jnp.bfloat16))


def shards(
    asking_vectors_matrix,
    matched_keys_matrix,
    carried_vectors_matrix,
    upstream_cotangent,
    w_out,
    panel_entry_offsets,
    rightward_panel_per_entry,
):
    nodes_here = asking_vectors_matrix.shape[1]
    width = asking_vectors_matrix.shape[2]
    n_seq = lax.axis_size("seq")
    nodes = nodes_here * n_seq
    grad_here = upstream_cotangent[0]
    grad_full = lax.all_gather(grad_here, "seq", axis=0, tiled=True)
    w_full = lax.all_gather(w_out, "seq", axis=0, tiled=True)
    stacked = jnp.stack(
        [asking_vectors_matrix[0], matched_keys_matrix[0], carried_vectors_matrix[0]]
    ).reshape(3, nodes_here, H, HD)
    heads = lax.all_to_all(stacked, "seq", split_axis=2, concat_axis=1, tiled=True)
    q_heads, k_heads, v_heads = (heads[0], heads[1], heads[2])
    local_heads = q_heads.shape[1]
    allowed = tile_mask(panel_entry_offsets[0], rightward_panel_per_entry[0], nodes)
    g_flat = lax.dot_general(
        grad_full, w_out, (((1,), (1,)), ((), ())), preferred_element_type=jnp.float32
    ).astype(jnp.bfloat16)
    g_heads = g_flat.reshape(nodes, local_heads, HD)
    attended, expd, row_total = attend(q_heads, k_heads, v_heads, g_heads, allowed)
    returned = lax.all_to_all(attended, "seq", split_axis=0, concat_axis=1, tiled=True)
    attended_nodes = returned.reshape(nodes_here, width)
    layer_out = jnp.dot(attended_nodes, w_full, preferred_element_type=jnp.float32)
    layer_out = layer_out.astype(jnp.bfloat16)[None]
    att_blocks = attended.reshape(n_seq, nodes_here, local_heads * HD)
    grad_blocks = grad_full.reshape(n_seq, nodes_here, width)
    terms = jnp.einsum(
        "bnf,bnk->bfk", att_blocks, grad_blocks, preferred_element_type=jnp.float32
    ).astype(jnp.bfloat16)
    w_rows = jnp.sum(terms.astype(jnp.float32), axis=0)
    batch = asking_vectors_matrix.shape[0] * lax.axis_size("dp")
    w_out_grad = lax.psum(w_rows, "dp") / batch
    q_g, k_g, v_g = attend_back(q_heads, k_heads, v_heads, g_heads, attended, expd, row_total)
    grads = jnp.stack([q_g, k_g, v_g])
    back = lax.all_to_all(grads, "seq", split_axis=1, concat_axis=2, tiled=True)
    back = back.reshape(3, 1, nodes_here, width)
    return (layer_out, back[0], back[1], back[2], w_out_grad)


def solution(mesh):
    return jax.shard_map(
        shards,
        mesh=mesh,
        in_specs=(
            P("dp", "seq", None),
            P("dp", "seq", None),
            P("dp", "seq", None),
            P("dp", "seq", None),
            P("seq", None),
            P("dp", None),
            P("dp", None),
        ),
        out_specs=(
            P("dp", "seq", None),
            P("dp", "seq", None),
            P("dp", "seq", None),
            P("dp", "seq", None),
            P("seq", None),
        ),
        check_vma=False,
    )
```

profile of v0, /device:TPU:0, one launch (start us, length us, event | category | flops | bytes accessed | tf_op | source)
XLA Modules:
  0.0 276.4 jit_solution(7157705828374576800)
XLA Ops:
  7.2 0.7 all-gather.6.cloned.1.call-update
  7.9 1.3 copy.117
  9.2 1.3 copy.118
  10.5 1.3 copy.119
  12.1 1.2 copy.120
  13.3 6.3 %all-to-all-start = ((bf16[3,128,16,128]{1,3,0,2:T(8,128)(2,1)}), bf16[3,128,16,128]{1,3,0,2:T(8,128)(2,1)S(1)}, u32[]{:S(2)}, u32[]{:S(2)}) async-start(bf16[3,128,16,128]{1,3,0,2:T(8,128)(2,1)} %copy.120), calls=%async_computation | async-start | bytes 3145728 | tf_op jit(solution)/shard_map/all_to_all | solution.py:73
  20.5 1.5 copy.157
  22.0 69.1 %all-to-all-done = bf16[3,128,16,128]{1,3,0,2:T(8,128)(2,1)S(1)} async-done(((bf16[3,128,16,128]{1,3,0,2:T(8,128)(2,1)}), bf16[3,128,16,128]{1,3,0,2:T(8,128)(2,1)S(1)}, u32[]{:S(2)}, u32[]{:S(2)}) %all-to-all-start) | async-done | bytes 1572896 | tf_op jit(solution)/shard_map/all_to_all | solution.py:73
  91.2 0.9 copy.121
  92.9 7.1 %fusion.44 = (f32[2,1024]{1,0:T(2,128)S(1)}, f32[2,1024,1024]{1,2,0:T(8,128)}) fusion(pred[1024,1024]{0,1:T(8,128)(4,1)} %bitcast.89, bf16[1024,2,128]{2,0,1:T(8,128)(2,1)S(1)} %bitcast.86, bf16[1024,2,128]{2,0,1:T(8,128)(2,1)S(1)} %bitcast.82), kind=kOutput, calls=%fused_computation.48 | convolution fusion | flops 1086325760 | bytes 10493952 | tf_op jit(solution)/shard_map/sub | solution.py:30
  100.0 3.5 %fusion.27 = bf16[1024,256]{0,1:T(8,128)(2,1)S(1)} fusion(bf16[256,2048]{1,0:T(8,128)(2,1)S(1)} %copy-done, bf16[1,1024,2048]{2,1,0:T(8,128)(2,1)} %all-gather.6.cloned.1.call-done), kind=kOutput, calls=%fused_computation.28 | convolution fusion | flops 1074003968 | bytes 5767168 | tf_op jit(solution)/shard_map/dot_general | solution.py:77
  103.5 4.5 %multiply_reduce_fusion = (f32[1024,2]{0,1:T(2,128)S(1)}, bf16[1024,2,128]{0,2,1:T(8,128)(2,1)S(1)}) fusion(bf16[1024,256]{0,1:T(8,128)(2,1)S(1)} %fusion.27, f32[1024,2]{0,1:T(2,128)S(1)} %bitcast.93, bf16[1024,2,128]{0,2,1:T(8,128)(2,1)S(1)} %squeeze.22, f32[2,1024,1024]{1,2,0:T(8,128)} %get-tuple-element.12), kind=kOutput, calls=%fused_computation.34 | convolution fusion | flops 540538880 | bytes 9977856 | tf_op jit(solution)/shard_map/hij,jhd->ihd/dot_general | solution.py:32
  108.3 3.6 %convert_reduce_fusion = f32[256,2048]{1,0:T(8,128)} fusion(bf16[8,128,2048]{2,1,0:T(8,128)(2,1)S(1)} %bitcast.95, bf16[8,128,256]{1,0,2:T(8,128)(2,1)S(1)} %bitcast.92), kind=kOutput, calls=%fused_computation.1 | convolution fusion | flops 1085800448 | bytes 6815744 | tf_op jit(solution)/shard_map/bnf,bnk->bfk/dot_general | solution.py:88
  112.0 0.7 all-gather.4.cloned.1.call-update
  112.7 1.1 copy.127
  113.8 3.7 %all-to-all-start.1 = ((bf16[1024,2,128]{2,1,0:T(2,128)(2,1)}), bf16[1024,2,128]{2,1,0:T(2,128)(2,1)S(1)}, u32[]{:S(2)}, u32[]{:S(2)}) async-start(bf16[1024,2,128]{2,1,0:T(2,128)(2,1)} %copy.127), calls=%async_computation.1 | async-start | bytes 1048576 | tf_op jit(solution)/shard_map/all_to_all | solution.py:82
  117.5 4.3 %multiply_convert_fusion = bf16[2,1024,1024]{1,2,0:T(8,128)(2,1)S(1)} fusion(f32[2,1024]{1,0:T(2,128)S(1)} %bitcast.94, f32[2,1024,1024]{1,2,0:T(8,128)} %get-tuple-element.12, f32[2,1024]{1,0:T(2,128)S(1)} %get-tuple-element.11, bf16[1024,2,128]{0,2,1:T(8,128)(2,1)S(1)} %bitcast.90, bf16[1024,2,128]{0,2,1:T(8,128)(2,1)S(1)} %squeeze.22), kind=kOutput, calls=%fused_computation.2 | convolution fusion | flops 547356672 | bytes 13647872 | tf_op jit(solution)/shard_map/ihd,jhd->hij/dot_general | solution.py:45
  121.8 0.8 fusion.30
  122.6 1.6 fusion.31
  124.2 5.0 %fusion.32 = bf16[1,1024,2,128]{1,3,2,0:T(8,128)(2,1)S(1)} fusion(bf16[1024,2,128]{0,2,1:T(8,128)(2,1)S(1)} %bitcast.91, f32[2,1024,1024]{1,2,0:T(8,128)} %get-tuple-element.12, f32[2,1024]{1,0:T(2,128)S(1)} %get-tuple-element.11), kind=kOutput, calls=%fused_computation.31 | convolution fusion | flops 541327360 | bytes 9445376 | tf_op jit(solution)/shard_map/hij,ihd->jhd/dot_general | solution.py:44
  129.4 3.0 %copy.138 = bf16[3,1024,2,128]{3,2,0,1:T(2,128)(2,1)} copy(bf16[3,1024,2,128]{1,3,2,0:T(8,128)(2,1)S(1)} %pad_maximum_fusion.1) | data formatting | bytes 3145728 | tf_op jit(solution)/shard_map/stack | solution.py:95
  132.6 4.6 %all-to-all-start.2 = ((bf16[3,1024,2,128]{3,2,0,1:T(2,128)(2,1)}), bf16[3,1024,2,128]{3,2,0,1:T(2,128)(2,1)S(1)}, u32[]{:S(2)}, u32[]{:S(2)}) async-start(bf16[3,1024,2,128]{3,2,0,1:T(2,128)(2,1)} %copy.138), calls=%async_computation.2 | async-start | bytes 3145728 | tf_op jit(solution)/shard_map/all_to_all | solution.py:96
  137.6 43.1 %all-reduce.2.cloned.1.call-done = f32[256,2048]{1,0:T(8,128)} async-done(((f32[256,2048]{1,0:T(8,128)}), f32[256,2048]{1,0:T(8,128)}) %all-reduce.2.cloned.1.call-update) | async-done | bytes 2097168 | tf_op jit(solution)/shard_map/psum | solution.py:93
  180.7 3.1 %broadcast_multiply_fusion = f32[256,2048]{1,0:T(8,128)} fusion(f32[256,2048]{1,0:T(8,128)} %all-reduce.2.cloned.1.call-done), kind=kLoop, calls=%fused_computation.33 | loop fusion | flops 524288 | bytes 4194304 | tf_op jit(solution)/shard_map/div | solution.py:93
  183.8 1.2 fusion.42
  185.0 0.4 copy.139
  185.4 1.2 squeeze.26
  186.6 0.4 copy.140
  186.9 1.2 squeeze.27
  188.5 1.2 squeeze.28
  189.7 74.8 %all-gather.4.cloned.1.call-done = bf16[2048,2048]{1,0:T(8,128)(2,1)} async-done(((bf16[256,2048]{1,0:T(8,128)(2,1)}), bf16[2048,2048]{1,0:T(8,128)(2,1)}) %all-gather.4.cloned.1.call-update) | async-done | bytes 8388624 | tf_op jit(solution)/shard_map/all_gather | solution.py:69
  264.5 5.5 %fusion.14 = bf16[1,128,2048]{2,1,0:T(8,128)(2,1)} fusion(bf16[128,2048]{0,1:T(8,128)(2,1)S(1)} %bitcast.84, bf16[2048,2048]{1,0:T(8,128)(2,1)} %all-gather.4.cloned.1.call-done), kind=kOutput, calls=%fused_computation.19 | convolution fusion | flops 1074003968 | bytes 9437184 | tf_op jit(solution)/shard_map/dot_general | solution.py:84
  (35 shorter events, 3.3 us)
Async XLA Ops:
  7.2 92.9 %all-gather.6.cloned.1.call-start = ((), (), s32[]{:S(2)}) async-start(), calls=%async_computation.5 | async-start | bytes 4718592 | tf_op jit(solution)/shard_map/all_gather | solution.py:68
  11.9 7.8 %copy-start.4 = (s32[1,9]{1,0:T(1,128)S(1)}, s32[1,9]{1,0:T(1,128)}, u32[]{:S(2)}) copy-start(s32[1,9]{1,0:T(1,128)} %param.12) | copy-start | bytes 112
  11.9 8.0 %copy-start.5 = (s32[1,32]{1,0:T(1,128)S(1)}, s32[1,32]{1,0:T(1,128)}, u32[]{:S(2)}) copy-start(s32[1,32]{1,0:T(1,128)} %param.13) | copy-start | bytes 388
  13.3 77.9 %all-to-all-start = ((bf16[3,128,16,128]{1,3,0,2:T(8,128)(2,1)}), bf16[3,128,16,128]{1,3,0,2:T(8,128)(2,1)S(1)}, u32[]{:S(2)}, u32[]{:S(2)}) async-start(bf16[3,128,16,128]{1,3,0,2:T(8,128)(2,1)} %copy.120), calls=%async_computation | async-start | bytes 3145728 | tf_op jit(solution)/shard_map/all_to_all | solution.py:73
  19.6 161.0 %all-reduce.2.cloned.1.call-start = ((), (), s32[]{:S(2)}) async-start(), calls=%async_computation.4 | async-start | bytes 4194304 | tf_op jit(solution)/shard_map/psum | solution.py:93
  92.9 7.2 %copy-start = (bf16[256,2048]{1,0:T(8,128)(2,1)S(1)}, bf16[256,2048]{1,0:T(8,128)(2,1)}, u32[]{:S(2)}) copy-start(bf16[256,2048]{1,0:T(8,128)(2,1)} %param.11) | copy-start | bytes 3145732
  103.5 4.5 %copy-start.1 = (bf16[1024,256]{0,1:T(8,128)(2,1)}, bf16[1024,256]{0,1:T(8,128)(2,1)S(1)}, u32[]{:S(2)}) copy-start(bf16[1024,256]{0,1:T(8,128)(2,1)S(1)} %fusion.27) | copy-start | bytes 1572868
  103.5 4.8 %copy-start.3 = (bf16[1,1024,2048]{2,1,0:T(8,128)(2,1)S(1)}, bf16[1,1024,2048]{2,1,0:T(8,128)(2,1)}, u32[]{:S(2)}) copy-start(bf16[1,1024,2048]{2,1,0:T(8,128)(2,1)} %all-gather.6.cloned.1.call-done) | copy-start | bytes 12582916
  111.9 5.6 %copy-start.2 = (bf16[1024,256]{0,1:T(8,128)(2,1)S(1)}, bf16[1024,256]{0,1:T(8,128)(2,1)}, u32[]{:S(2)}) copy-start(bf16[1024,256]{0,1:T(8,128)(2,1)} %copy-done.1) | copy-start | bytes 1572868
  111.9 152.5 %all-gather.4.cloned.1.call-start = ((), (), s32[]{:S(2)}) async-start(), calls=%async_computation.3 | async-start | bytes 9437184 | tf_op jit(solution)/shard_map/all_gather | solution.py:69
  113.8 18.8 %all-to-all-start.1 = ((bf16[1024,2,128]{2,1,0:T(2,128)(2,1)}), bf16[1024,2,128]{2,1,0:T(2,128)(2,1)S(1)}, u32[]{:S(2)}, u32[]{:S(2)}) async-start(bf16[1024,2,128]{2,1,0:T(2,128)(2,1)} %copy.127), calls=%async_computation.1 | async-start | bytes 1048576 | tf_op jit(solution)/shard_map/all_to_all | solution.py:82
  132.6 51.2 %all-to-all-start.2 = ((bf16[3,1024,2,128]{3,2,0,1:T(2,128)(2,1)}), bf16[3,1024,2,128]{3,2,0,1:T(2,128)(2,1)S(1)}, u32[]{:S(2)}, u32[]{:S(2)}) async-start(bf16[3,1024,2,128]{3,2,0,1:T(2,128)(2,1)} %copy.138), calls=%async_computation.2 | async-start | bytes 3145728 | tf_op jit(solution)/shard_map/all_to_all | solution.py:96
Sparse Core Ops, SparseCore 0:
  9.6 83.0 all-gather.5
  112.1 68.5 all-reduce.1
  182.4 82.0 all-gather.3
where the time goes:
time: 277 us; the launch traced here: 276 us
  waiting for transfers between devices  189 us (68%)
  matrix products  36.1 us (13%)
  local copies, waits for them, and re-layouts  19.5 us (7%)
  starting transfers between devices  14.8 us (5%)
  between operations  14 us (5%)
  other arithmetic  3.58 us (1%)
    all_gather x1, waiting for transfers between devices, shards(): w_full = lax.all_gather(w_out, 'seq', axis=0, tiled=True)  74.8 us
    all_to_all x1, waiting for transfers between devices, shards(): lax.all_to_all(stacked, 'seq', split_axis=2, concat_axis=1, tiled=True)  69.1 us
    psum x1, waiting for transfers between devices, shards(): w_out_grad = lax.psum(w_rows, 'dp') / batch  43.1 us
    sub x1, matrix products, attend(): expd = jnp.where(allowed[None], jnp.exp(scores - row_max), 0.0)  7.15 us
    all_to_all x1, starting transfers between devices, shards(): lax.all_to_all(stacked, 'seq', split_axis=2, concat_axis=1, tiled=True)  6.33 us
    unnamed x17, local copies, waits for them, and re-layouts  5.75 us
  transfers between devices with their start and end apart: 6, of which 4 were waited for; matrix products, arithmetic and copies ran while one was open for 15% of the time, Pallas kernels for 0%

commit v1 on v0

--- a/solution.py
+++ b/solution.py
@@ -6,6 +6,18 @@
 
 H = 16
 HD = 128
+
+
+def split_up(x, dim, size):
+    dims = x.shape
+    blocks = x.reshape(*dims[:dim], size, dims[dim] // size, *dims[dim + 1 :])
+    return jnp.moveaxis(blocks, dim, 0)
+
+
+def laid_out(blocks, dim):
+    shape = list(blocks.shape[1:])
+    shape[dim] *= blocks.shape[0]
+    return jnp.moveaxis(blocks, 0, dim).reshape(shape)
 
 
 def tile_mask(starts, columns, nodes):
@@ -70,7 +82,14 @@
     stacked = jnp.stack(
         [asking_vectors_matrix[0], matched_keys_matrix[0], carried_vectors_matrix[0]]
     ).reshape(3, nodes_here, H, HD)
-    heads = lax.all_to_all(stacked, "seq", split_axis=2, concat_axis=1, tiled=True)
+    devices, mine = (lax.axis_size("seq"), lax.axis_index("seq"))
+    blocks = split_up(stacked, 2, devices)
+    outs = [blocks[mine]]
+    for step in range(1, devices):
+        sent = blocks[mine ^ step]
+        outs.append(lax.ppermute(sent, "seq", [(i, i ^ step) for i in range(devices)]))
+    blocks = jnp.stack(outs)[mine ^ jnp.arange(devices)]
+    heads = laid_out(blocks, 1)
     q_heads, k_heads, v_heads = (heads[0], heads[1], heads[2])
     local_heads = q_heads.shape[1]
     allowed = tile_mask(panel_entry_offsets[0], rightward_panel_per_entry[0], nodes)

time: 277 us -> 275 us (level)
  waiting for transfers between devices: 189 us -> 174 us
  starting transfers between devices: 14.8 us -> 24.9 us
    all_to_all x1 -> x0, waiting for transfers between devices: 69.1 us -> none  [shards(): lax.all_to_all(stacked, 'seq', split_axis=2, concat_axis=1, tiled=True)]
    ppermute x0 -> x7, waiting for transfers between devices: none -> 38.7 us  [shards(): lax.ppermute(sent, 'seq', [(i, i ^ step) for i in range(devices)])]
    all_gather x1, waiting for transfers between devices: 0.01 us -> 15.3 us  [shards(): grad_full = lax.all_gather(grad_here, 'seq', axis=0, tiled=True)]
    ppermute x0 -> x7, starting transfers between devices: none -> 9.69 us  [shards(): lax.ppermute(sent, 'seq', [(i, i ^ step) for i in range(devices)])]
    all_to_all x1, starting transfers between devices: 3.71 us -> 10.4 us  [shards(): lax.all_to_all(attended, 'seq', split_axis=0, concat_axis=1, tiled=True)]
    all_to_all x1 -> x0, starting transfers between devices: 6.33 us -> none  [shards(): lax.all_to_all(stacked, 'seq', split_axis=2, concat_axis=1, tiled=True)]
    unnamed x17 -> x28, local copies, waits for them, and re-layouts: 5.75 us -> 4.47 us
  transfers between devices with their start and end apart: 6 -> 12, of which waited for: 4 -> 9; matrix products, arithmetic and copies ran while one was open for 15% -> 16% of each run, Pallas kernels for 0% -> 0%
where the time goes in v1:
time: 275 us; the launch traced here: 274 us
  waiting for transfers between devices  174 us (63%)
  matrix products  36.1 us (13%)
  starting transfers between devices  24.9 us (9%)
  local copies, waits for them, and re-layouts  19.5 us (7%)
  between operations  14.1 us (5%)
  other arithmetic  4.95 us (2%)
    all_gather x1, waiting for transfers between devices, shards(): w_full = lax.all_gather(w_out, 'seq', axis=0, tiled=True)  74.8 us
    psum x1, waiting for transfers between devices, shards(): w_out_grad = lax.psum(w_rows, 'dp') / batch  43.9 us
    ppermute x7, waiting for transfers between devices, shards(): lax.ppermute(sent, 'seq', [(i, i ^ step) for i in range(devices)])  38.7 us
    all_gather x1, waiting for transfers between devices, shards(): grad_full = lax.all_gather(grad_here, 'seq', axis=0, tiled=True)  15.3 us
    all_to_all x1, starting transfers between devices, shards(): lax.all_to_all(attended, 'seq', split_axis=0, concat_axis=1, tiled=True)  10.4 us
    ppermute x7, starting transfers between devices, shards(): lax.ppermute(sent, 'seq', [(i, i ^ step) for i in range(devices)])  9.69 us
    sub x1, matrix products, attend(): expd = jnp.where(allowed[None], jnp.exp(scores - row_max), 0.0)  7.13 us
  transfers between devices with their start and end apart: 12, of which 9 were waited for; matrix products, arithmetic and copies ran while one was open for 16% of the time, Pallas kernels for 0%

profile of v1, /device:TPU:0, one launch (start us, length us, event | category | flops | bytes accessed | tf_op | source)
XLA Modules:
  0.0 274.1 jit_solution(10986695980167896737)
XLA Ops:
  8.0 1.5 pad_maximum_fusion
  9.5 1.1 reshape_reshape.3
  10.7 1.4 constant_dynamic-slice_fusion
  14.0 2.6 collective-permute-start.1
  16.8 2.8 %collective-permute-start.3 = (bf16[3,128,2,128]{3,1,2,0:T(8,128)(2,1)S(1)}, bf16[3,128,2,128]{3,1,2,0:T(8,128)(2,1)S(1)}, u32[]{:S(2)}, u32[]{:S(2)}) collective-permute-start(bf16[3,128,2,128]{3,1,2,0:T(8,128)(2,1)S(1)} %bitcast.133), channel_id=1, source_target_pairs={{0,4},{1,5},{2,6},{3,7},{4,0},{5,1},{6,2},{7,3},{8,12},{9,13},{10,... | collective-permute-start | bytes 589832 | tf_op jit(solution)/shard_map/ppermute | solution.py:90
  20.7 1.5 copy.170
  22.2 3.6 %collective-permute-start.5 = (bf16[3,128,2,128]{3,1,2,0:T(8,128)(2,1)S(1)}, bf16[3,128,2,128]{3,1,2,0:T(8,128)(2,1)S(1)}, u32[]{:S(2)}, u32[]{:S(2)}) collective-permute-start(bf16[3,128,2,128]{3,1,2,0:T(8,128)(2,1)S(1)} %bitcast.131), channel_id=1, source_target_pairs={{0,6},{1,7},{2,4},{3,5},{4,2},{5,3},{6,0},{7,1},{8,14},{9,15},{10,... | collective-permute-start | bytes 589832 | tf_op jit(solution)/shard_map/ppermute | solution.py:90
  26.8 6.9 %collective-permute-done.1 = bf16[3,128,2,128]{3,1,2,0:T(8,128)(2,1)S(1)} collective-permute-done((bf16[3,128,2,128]{3,1,2,0:T(8,128)(2,1)}, bf16[3,128,2,128]{3,1,2,0:T(8,128)(2,1)S(1)}, u32[]{:S(2)}, u32[]{:S(2)}) %collective-permute-start.1) | collective-permute-done | bytes 196640 | tf_op jit(solution)/shard_map/ppermute | solution.py:90
  33.7 10.2 %collective-permute-done.2 = bf16[3,128,2,128]{3,1,2,0:T(8,128)(2,1)S(1)} collective-permute-done((bf16[3,128,2,128]{3,1,2,0:T(8,128)(2,1)S(1)}, bf16[3,128,2,128]{3,1,2,0:T(8,128)(2,1)S(1)}, u32[]{:S(2)}, u32[]{:S(2)}) %collective-permute-start.2) | collective-permute-done | bytes 196640 | tf_op jit(solution)/shard_map/ppermute | solution.py:90
  44.0 4.5 %collective-permute-done.4 = bf16[3,128,2,128]{3,1,2,0:T(8,128)(2,1)S(1)} collective-permute-done((bf16[3,128,2,128]{3,1,2,0:T(8,128)(2,1)S(1)}, bf16[3,128,2,128]{3,1,2,0:T(8,128)(2,1)S(1)}, u32[]{:S(2)}, u32[]{:S(2)}) %collective-permute-start.4) | collective-permute-done | bytes 196640 | tf_op jit(solution)/shard_map/ppermute | solution.py:90
  48.5 10.3 %collective-permute-done.5 = bf16[3,128,2,128]{3,1,2,0:T(8,128)(2,1)S(1)} collective-permute-done((bf16[3,128,2,128]{3,1,2,0:T(8,128)(2,1)S(1)}, bf16[3,128,2,128]{3,1,2,0:T(8,128)(2,1)S(1)}, u32[]{:S(2)}, u32[]{:S(2)}) %collective-permute-start.5) | collective-permute-done | bytes 196640 | tf_op jit(solution)/shard_map/ppermute | solution.py:90
  58.8 6.9 %collective-permute-done.6 = bf16[3,128,2,128]{3,1,2,0:T(8,128)(2,1)S(1)} collective-permute-done((bf16[3,128,2,128]{3,1,2,0:T(8,128)(2,1)S(1)}, bf16[3,128,2,128]{3,1,2,0:T(8,128)(2,1)S(1)}, u32[]{:S(2)}, u32[]{:S(2)}) %collective-permute-start.6) | collective-permute-done | bytes 196640 | tf_op jit(solution)/shard_map/ppermute | solution.py:90
  67.4 7.1 %fusion.46 = (f32[2,1024]{1,0:T(2,128)S(1)}, f32[2,1024,1024]{1,2,0:T(8,128)}) fusion(pred[1024,1024]{0,1:T(8,128)(4,1)} %bitcast.126, bf16[1024,2,128]{2,0,1:T(8,128)(2,1)S(1)} %bitcast.123, bf16[1024,2,128]{2,0,1:T(8,128)(2,1)S(1)} %bitcast.119), kind=kOutput, calls=%fused_computation.76 | convolution fusion | flops 1086325760 | bytes 10493952 | tf_op jit(solution)/shard_map/sub | solution.py:42
  74.5 15.3 %all-gather.6.cloned.1.call-done = bf16[1,1024,2048]{2,1,0:T(8,128)(2,1)} async-done(((bf16[1,128,2048]{2,1,0:T(8,128)(2,1)}), bf16[1,1024,2048]{2,1,0:T(8,128)(2,1)}) %all-gather.6.cloned.1.call-update) | async-done | bytes 4194320 | tf_op jit(solution)/shard_map/all_gather | solution.py:80
  89.8 3.5 %fusion.27 = bf16[1024,256]{0,1:T(8,128)(2,1)S(1)} fusion(bf16[256,2048]{1,0:T(8,128)(2,1)S(1)} %copy-done, bf16[1,1024,2048]{2,1,0:T(8,128)(2,1)} %all-gather.6.cloned.1.call-done), kind=kOutput, calls=%fused_computation.29 | convolution fusion | flops 1074003968 | bytes 5767168 | tf_op jit(solution)/shard_map/dot_general | solution.py:96
  93.3 4.5 %multiply_reduce_fusion = (f32[1024,2]{0,1:T(2,128)S(1)}, bf16[1024,2,128]{0,2,1:T(8,128)(2,1)S(1)}) fusion(bf16[1024,256]{0,1:T(8,128)(2,1)S(1)} %fusion.27, f32[1024,2]{0,1:T(2,128)S(1)} %bitcast.135, bf16[1024,2,128]{0,2,1:T(8,128)(2,1)S(1)} %squeeze.50, f32[2,1024,1024]{1,2,0:T(8,128)} %get-tuple-element.20), kind=kOutput, calls=%fused_computation.35 | convolution fusion | flops 540538880 | bytes 9977856 | tf_op jit(solution)/shard_map/hij,jhd->ihd/dot_general | solution.py:44
  98.0 3.6 %convert_reduce_fusion = f32[256,2048]{1,0:T(8,128)} fusion(bf16[8,128,2048]{2,1,0:T(8,128)(2,1)S(1)} %bitcast.137, bf16[8,128,256]{1,0,2:T(8,128)(2,1)S(1)} %bitcast.129), kind=kOutput, calls=%fused_computation.2 | convolution fusion | flops 1085800448 | bytes 6815744 | tf_op jit(solution)/shard_map/bnf,bnk->bfk/dot_general | solution.py:107
  102.4 1.1 copy.122
  103.5 10.4 %all-to-all-start = ((bf16[1024,2,128]{2,1,0:T(2,128)(2,1)}), bf16[1024,2,128]{2,1,0:T(2,128)(2,1)S(1)}, u32[]{:S(2)}, u32[]{:S(2)}) async-start(bf16[1024,2,128]{2,1,0:T(2,128)(2,1)} %copy.122), calls=%async_computation | async-start | bytes 1048576 | tf_op jit(solution)/shard_map/all_to_all | solution.py:101
  114.0 4.4 %multiply_convert_fusion = bf16[2,1024,1024]{1,2,0:T(8,128)(2,1)S(1)} fusion(f32[2,1024]{1,0:T(2,128)S(1)} %bitcast.136, f32[2,1024,1024]{1,2,0:T(8,128)} %get-tuple-element.20, f32[2,1024]{1,0:T(2,128)S(1)} %get-tuple-element.19, bf16[1024,2,128]{0,2,1:T(8,128)(2,1)S(1)} %bitcast.127, bf16[1024,2,128]{0,2,1:T(8,128)(2,1)S(1)} %squeeze.50), kind=kOutput, calls=%fused_computation.3 | convolution fusion | flops 547356672 | bytes 13647872 | tf_op jit(solution)/shard_map/ihd,jhd->hij/dot_general | solution.py:57
  119.2 1.5 fusion.31
  120.7 5.0 %fusion.32 = bf16[1,1024,2,128]{1,3,2,0:T(8,128)(2,1)S(1)} fusion(bf16[1024,2,128]{0,2,1:T(8,128)(2,1)S(1)} %bitcast.128, f32[2,1024,1024]{1,2,0:T(8,128)} %get-tuple-element.20, f32[2,1024]{1,0:T(2,128)S(1)} %get-tuple-element.19), kind=kOutput, calls=%fused_computation.32 | convolution fusion | flops 541327360 | bytes 9445376 | tf_op jit(solution)/shard_map/hij,ihd->jhd/dot_general | solution.py:56
  125.9 3.1 %copy.133 = bf16[3,1024,2,128]{3,2,0,1:T(2,128)(2,1)} copy(bf16[3,1024,2,128]{1,3,2,0:T(8,128)(2,1)S(1)} %pad_maximum_fusion.1) | data formatting | bytes 3145728 | tf_op jit(solution)/shard_map/stack | solution.py:114
  129.3 4.7 %all-to-all-start.1 = ((bf16[3,1024,2,128]{3,2,0,1:T(2,128)(2,1)}), bf16[3,1024,2,128]{3,2,0,1:T(2,128)(2,1)S(1)}, u32[]{:S(2)}, u32[]{:S(2)}) async-start(bf16[3,1024,2,128]{3,2,0,1:T(2,128)(2,1)} %copy.133), calls=%async_computation.1 | async-start | bytes 3145728 | tf_op jit(solution)/shard_map/all_to_all | solution.py:115
  134.4 43.9 %all-reduce.2.cloned.1.call-done = f32[256,2048]{1,0:T(8,128)} async-done(((f32[256,2048]{1,0:T(8,128)}), f32[256,2048]{1,0:T(8,128)}) %all-reduce.2.cloned.1.call-update) | async-done | bytes 2097168 | tf_op jit(solution)/shard_map/psum | solution.py:112
  178.3 3.1 %broadcast_multiply_fusion = f32[256,2048]{1,0:T(8,128)} fusion(f32[256,2048]{1,0:T(8,128)} %all-reduce.2.cloned.1.call-done), kind=kLoop, calls=%fused_computation.34 | loop fusion | flops 524288 | bytes 4194304 | tf_op jit(solution)/shard_map/div | solution.py:112
  181.4 1.2 fusion.44
  183.0 1.2 squeeze.54
  184.6 1.2 squeeze.55
  186.1 1.2 squeeze.56
  187.3 74.8 %all-gather.4.cloned.1.call-done = bf16[2048,2048]{1,0:T(8,128)(2,1)} async-done(((bf16[256,2048]{1,0:T(8,128)(2,1)}), bf16[2048,2048]{1,0:T(8,128)(2,1)}) %all-gather.4.cloned.1.call-update) | async-done | bytes 8388624 | tf_op jit(solution)/shard_map/all_gather | solution.py:81
  262.1 5.5 %fusion.14 = bf16[1,128,2048]{2,1,0:T(8,128)(2,1)} fusion(bf16[128,2048]{0,1:T(8,128)(2,1)S(1)} %bitcast.121, bf16[2048,2048]{1,0:T(8,128)(2,1)} %all-gather.4.cloned.1.call-done), kind=kOutput, calls=%fused_computation.20 | convolution fusion | flops 1074003968 | bytes 9437184 | tf_op jit(solution)/shard_map/dot_general | solution.py:103
  (62 shorter events, 10.5 us)
Async XLA Ops:
  7.2 82.6 %all-gather.6.cloned.1.call-start = ((), (), s32[]{:S(2)}) async-start(), calls=%async_computation.4 | async-start | bytes 4718592 | tf_op jit(solution)/shard_map/all_gather | solution.py:80
  7.9 170.4 %all-reduce.2.cloned.1.call-start = ((), (), s32[]{:S(2)}) async-start(), calls=%async_computation.3 | async-start | bytes 4194304 | tf_op jit(solution)/shard_map/psum | solution.py:112
  9.5 10.3 %copy-start.4 = (s32[1,9]{1,0:T(1,128)S(1)}, s32[1,9]{1,0:T(1,128)}, u32[]{:S(2)}) copy-start(s32[1,9]{1,0:T(1,128)} %param.12) | copy-start | bytes 112
  9.5 10.4 %copy-start.5 = (s32[1,32]{1,0:T(1,128)S(1)}, s32[1,32]{1,0:T(1,128)}, u32[]{:S(2)}) copy-start(s32[1,32]{1,0:T(1,128)} %param.13) | copy-start | bytes 388
  12.8 9.4 %collective-permute-start = (bf16[3,128,2,128]{3,1,2,0:T(8,128)(2,1)}, bf16[3,128,2,128]{3,1,2,0:T(8,128)(2,1)}, u32[]{:S(2)}, u32[]{:S(2)}) collective-permute-start(bf16[3,128,2,128]{3,1,2,0:T(8,128)(2,1)} %bitcast.115), channel_id=1, source_target_pairs={{0,1},{1,0},{2,3},{3,2},{4,5},{5,4},{6,7},{7,6},{8,9},{9,8},{10,11... | collective-permute-start | bytes 589832 | tf_op jit(solution)/shard_map/ppermute | solution.py:90
  14.0 19.7 %collective-permute-start.1 = (bf16[3,128,2,128]{3,1,2,0:T(8,128)(2,1)}, bf16[3,128,2,128]{3,1,2,0:T(8,128)(2,1)S(1)}, u32[]{:S(2)}, u32[]{:S(2)}) collective-permute-start(bf16[3,128,2,128]{3,1,2,0:T(8,128)(2,1)} %bitcast.114), channel_id=1, source_target_pairs={{0,2},{1,3},{2,0},{3,1},{4,6},{5,7},{6,4},{7,5},{8,10},{9,11},{10,... | collective-permute-start | bytes 589832 | tf_op jit(solution)/shard_map/ppermute | solution.py:90
  16.6 27.3 %collective-permute-start.2 = (bf16[3,128,2,128]{3,1,2,0:T(8,128)(2,1)S(1)}, bf16[3,128,2,128]{3,1,2,0:T(8,128)(2,1)S(1)}, u32[]{:S(2)}, u32[]{:S(2)}) collective-permute-start(bf16[3,128,2,128]{3,1,2,0:T(8,128)(2,1)S(1)} %bitcast.134), channel_id=1, source_target_pairs={{0,3},{1,2},{2,1},{3,0},{4,7},{5,6},{6,5},{7,4},{8,11},{9,10},{10,... | collective-permute-start | bytes 589832 | tf_op jit(solution)/shard_map/ppermute | solution.py:90
  16.8 27.1 %collective-permute-start.3 = (bf16[3,128,2,128]{3,1,2,0:T(8,128)(2,1)S(1)}, bf16[3,128,2,128]{3,1,2,0:T(8,128)(2,1)S(1)}, u32[]{:S(2)}, u32[]{:S(2)}) collective-permute-start(bf16[3,128,2,128]{3,1,2,0:T(8,128)(2,1)S(1)} %bitcast.133), channel_id=1, source_target_pairs={{0,4},{1,5},{2,6},{3,7},{4,0},{5,1},{6,2},{7,3},{8,12},{9,13},{10,... | collective-permute-start | bytes 589832 | tf_op jit(solution)/shard_map/ppermute | solution.py:90
  19.6 28.8 %collective-permute-start.4 = (bf16[3,128,2,128]{3,1,2,0:T(8,128)(2,1)S(1)}, bf16[3,128,2,128]{3,1,2,0:T(8,128)(2,1)S(1)}, u32[]{:S(2)}, u32[]{:S(2)}) collective-permute-start(bf16[3,128,2,128]{3,1,2,0:T(8,128)(2,1)S(1)} %bitcast.132), channel_id=1, source_target_pairs={{0,5},{1,4},{2,7},{3,6},{4,1},{5,0},{6,3},{7,2},{8,13},{9,12},{10,... | collective-permute-start | bytes 589832 | tf_op jit(solution)/shard_map/ppermute | solution.py:90
  22.2 36.6 %collective-permute-start.5 = (bf16[3,128,2,128]{3,1,2,0:T(8,128)(2,1)S(1)}, bf16[3,128,2,128]{3,1,2,0:T(8,128)(2,1)S(1)}, u32[]{:S(2)}, u32[]{:S(2)}) collective-permute-start(bf16[3,128,2,128]{3,1,2,0:T(8,128)(2,1)S(1)} %bitcast.131), channel_id=1, source_target_pairs={{0,6},{1,7},{2,4},{3,5},{4,2},{5,3},{6,0},{7,1},{8,14},{9,15},{10,... | collective-permute-start | bytes 589832 | tf_op jit(solution)/shard_map/ppermute | solution.py:90
  33.6 32.0 %collective-permute-start.6 = (bf16[3,128,2,128]{3,1,2,0:T(8,128)(2,1)S(1)}, bf16[3,128,2,128]{3,1,2,0:T(8,128)(2,1)S(1)}, u32[]{:S(2)}, u32[]{:S(2)}) collective-permute-start(bf16[3,128,2,128]{3,1,2,0:T(8,128)(2,1)S(1)} %bitcast.130), channel_id=1, source_target_pairs={{0,7},{1,6},{2,5},{3,4},{4,3},{5,2},{6,1},{7,0},{8,15},{9,14},{10,... | collective-permute-start | bytes 589832 | tf_op jit(solution)/shard_map/ppermute | solution.py:90
  67.4 22.4 %copy-start = (bf16[256,2048]{1,0:T(8,128)(2,1)S(1)}, bf16[256,2048]{1,0:T(8,128)(2,1)}, u32[]{:S(2)}) copy-start(bf16[256,2048]{1,0:T(8,128)(2,1)} %param.11) | copy-start | bytes 3145732
  93.3 4.5 %copy-start.1 = (bf16[1024,256]{0,1:T(8,128)(2,1)}, bf16[1024,256]{0,1:T(8,128)(2,1)S(1)}, u32[]{:S(2)}) copy-start(bf16[1024,256]{0,1:T(8,128)(2,1)S(1)} %fusion.27) | copy-start | bytes 1572868
  93.3 4.8 %copy-start.3 = (bf16[1,1024,2048]{2,1,0:T(8,128)(2,1)S(1)}, bf16[1,1024,2048]{2,1,0:T(8,128)(2,1)}, u32[]{:S(2)}) copy-start(bf16[1,1024,2048]{2,1,0:T(8,128)(2,1)} %all-gather.6.cloned.1.call-done) | copy-start | bytes 12582916
  101.7 12.3 %copy-start.2 = (bf16[1024,256]{0,1:T(8,128)(2,1)S(1)}, bf16[1024,256]{0,1:T(8,128)(2,1)}, u32[]{:S(2)}) copy-start(bf16[1024,256]{0,1:T(8,128)(2,1)} %copy-done.1) | copy-start | bytes 1572868
  101.7 160.4 %all-gather.4.cloned.1.call-start = ((), (), s32[]{:S(2)}) async-start(), calls=%async_computation.2 | async-start | bytes 9437184 | tf_op jit(solution)/shard_map/all_gather | solution.py:81
  103.5 25.8 %all-to-all-start = ((bf16[1024,2,128]{2,1,0:T(2,128)(2,1)}), bf16[1024,2,128]{2,1,0:T(2,128)(2,1)S(1)}, u32[]{:S(2)}, u32[]{:S(2)}) async-start(bf16[1024,2,128]{2,1,0:T(2,128)(2,1)} %copy.122), calls=%async_computation | async-start | bytes 1048576 | tf_op jit(solution)/shard_map/all_to_all | solution.py:101
  129.3 52.1 %all-to-all-start.1 = ((bf16[3,1024,2,128]{3,2,0,1:T(2,128)(2,1)}), bf16[3,1024,2,128]{3,2,0,1:T(2,128)(2,1)S(1)}, u32[]{:S(2)}, u32[]{:S(2)}) async-start(bf16[3,1024,2,128]{3,2,0,1:T(2,128)(2,1)} %copy.133), calls=%async_computation.1 | async-start | bytes 3145728 | tf_op jit(solution)/shard_map/all_to_all | solution.py:115
Sparse Core Ops, SparseCore 0:
  9.6 80.1 all-gather.5
  101.8 76.4 all-reduce.1
  180.0 82.0 all-gather.3
